TPU v7x, 32 devices: a whole 2x2x4 slice. The times are simulated.
32 devices in a mesh: pair: 8 (over z, y), virt: 4 (over x, core).
Axes of the slice: x: 2, y: 2, z: 4, core: 2. Of those that a mesh axis runs over, the one named last changes fastest.
Arguments:
- amps_pm: bfloat16 [64, 64, 4096], P(('pair', 'virt')), may hold values from -6 to 6
- integrals: bfloat16 [32, 4096, 2048], P(('pair', 'virt')), may hold values from -0.046875 to 0.046875
- fock_vv: bfloat16 [512, 512], replicated, may hold values from -0.25 to 0.25
- blk_tiles: int32 [32, 2], replicated, may hold values from 0 to 63, as said below
- blk_mask: int32 [32], replicated, may hold values 0 or 1
Outputs:
- sigma: bfloat16 [64, 64, 2048], P('pair', 'virt')
Inputs may be any that keep to these rules, and one draw needn't show every extreme that they name: Each row is (input tile pair, output tile pair). Integral tile r belongs to device r // 1 of the joined axis pair+virt, and its input tile pair lies in that device's virt slab: blk_tiles[r, 0] // 16 == (r) % 4. No two rows are equal.
All inputs are finite; a program needn't handle non-finite values.
Results may differ from a plain program's by a relative error of at most 0.0033.
Values may be sent and summed in bfloat16 or wider, within the bound.
No kernel may reach another device: no remote copies, remote signals or barrier semaphores. Data moves between devices by JAX's collectives and lax.ppermute only.
A program may use at most 128 MiB of HBM per device.

v0:
```python
import jax
import jax.numpy as jnp
from jax import lax
from jax.sharding import PartitionSpec as P

TILE = 64
NVT = 8
A_W = 8
AS = 32


def per_device(amps_pm, integrals, fock_vv, blk_tiles, blk_mask):
    n_virt = lax.axis_size("virt")
    n_pair = lax.axis_size("pair")
    pm_rows, n_tiles, tile_len = amps_pm.shape
    blk_dev = integrals.shape[0]
    out_cols = integrals.shape[2]
    slab = n_tiles // n_virt
    device = lax.axis_index(("pair", "virt"))
    virt_idx = lax.axis_index("virt")
    own_tiles = lax.dynamic_slice_in_dim(blk_tiles, device * blk_dev, blk_dev, 0)
    own_mask = lax.dynamic_slice_in_dim(blk_mask, device * blk_dev, blk_dev, 0).astype(jnp.float32)
    local_in = own_tiles[:, 0] - virt_idx * slab
    amps_vm = lax.all_to_all(amps_pm, "virt", split_axis=1, concat_axis=0, tiled=True)
    sub_rows = amps_pm[:, :, :out_cols].reshape(pm_rows, A_W, NVT, AS, TILE)
    fock_four = fock_vv.reshape(NVT, TILE, NVT, TILE)
    onebody = jnp.einsum(
        "pkqsd,bjqd->pkbsj", sub_rows, fock_four, preferred_element_type=jnp.float32
    )
    onebody = onebody.reshape(pm_rows, n_tiles, out_cols)
    arrived = lax.all_to_all(onebody, "virt", split_axis=1, concat_axis=0, tiled=True)
    chosen = jnp.take(lax.all_gather(amps_vm, "pair", axis=0, tiled=True), local_in, axis=1)
    product = jnp.einsum("rkc,kco->rko", chosen, integrals, preferred_element_type=jnp.float32)
    partial_value = product * own_mask[None, :, None]
    p_dev = partial_value.shape[0] // n_pair
    dest_virt = own_tiles[:, 1] // slab
    virt_ids = jnp.arange(n_virt, dtype=jnp.int32)
    select = (virt_ids[:, None] == dest_virt[None, :]).astype(jnp.float32)
    outgoing = (
        partial_value.reshape(n_pair, 1, p_dev, blk_dev, out_cols) * select[None, :, None, :, None]
    )
    outgoing = outgoing.reshape(n_pair * n_virt * p_dev, blk_dev, out_cols)
    received = lax.all_to_all(
        outgoing.astype(jnp.bfloat16), ("pair", "virt"), split_axis=0, concat_axis=1, tiled=True
    ).astype(outgoing.dtype)
    my_tiles = virt_idx * slab + jnp.arange(slab, dtype=jnp.int32)
    one_hot = (blk_tiles[:, 1][:, None] == my_tiles[None, :]).astype(jnp.float32)
    summed = jnp.einsum("pro,rt->pto", received, one_hot, precision=lax.Precision.HIGHEST)
    return (summed + arrived).astype(jnp.bfloat16)


def solution(mesh):
    return jax.shard_map(
        per_device,
        mesh=mesh,
        in_specs=(P(("pair", "virt"), None, None), P(("pair", "virt"), None, None), P(), P(), P()),
        out_specs=P("pair", "virt", None),
        check_vma=False,
    )
```

profile of v0, /device:TPU:0, one launch (start us, length us, event | category | flops | bytes accessed | tf_op | source)
XLA Modules:
  0.0 224.9 jit_solution(6049675598253406029)
XLA Ops:
  6.5 0.0 all-gather.2.cloned.1.call-start
  6.5 2.3 %copy.16 = bf16[2,64,4096]{2,0,1:T(2,128)(2,1)S(1)} copy(bf16[2,64,4096]{2,1,0:T(8,128)(2,1)} %param.5) | data formatting | bytes 2097152 | tf_op args[0]
  8.9 18.5 %all_to_all.54 = bf16[2,64,4096]{2,0,1:T(2,128)(2,1)S(1)} all-to-all(bf16[2,64,4096]{2,0,1:T(2,128)(2,1)S(1)} %copy.16), channel_id=1, replica_groups=mesh['pair'=8,'virt'=4] {'virt'}, dimensions={1} | all-to-all | bytes 2097152 | tf_op jit(solution)/shard_map/all_to_all | solution.py:24
  27.3 0.6 copy.17
  27.9 0.0 slice-start
  27.9 1.0 copy.18
  28.9 0.0 copy-start.1
  28.9 0.0 all-gather.2.cloned.1.call-update
  29.0 0.1 slice-done
  29.1 1.1 reshape.154
  30.2 0.0 copy-done.1
  30.2 0.5 reshape.111
  30.7 1.3 convolution_bitcast_fusion.1
  32.0 0.2 copy.30
  32.2 0.0 copy-start.2
  32.2 0.0 copy-start.3
  32.2 2.1 reshape.157
  34.3 3.5 %all-to-all-start.2 = ((f32[2,64,2048]{2,0,1:T(2,128)}), f32[2,64,2048]{2,0,1:T(2,128)S(1)}, u32[]{:S(2)}, u32[]{:S(2)}) async-start(f32[2,64,2048]{2,0,1:T(2,128)} %reshape.157), calls=%async_computation.2 | async-start | bytes 2097152 | tf_op jit(solution)/shard_map/all_to_all | solution.py:31
  37.9 0.0 copy-done.2
  37.9 0.1 constant_dynamic-slice_fusion.1
  38.0 0.5 fusion.22
  41.1 0.0 copy-done.3
  41.1 0.6 dynamic_slice.7
  43.0 0.1 mul.68
  43.1 0.1 mul.69
  43.2 110.7 %all-gather.2.cloned.1.call-done = bf16[64,16,4096]{2,1,0:T(8,128)(2,1)} async-done(((bf16[8,16,4096]{2,1,0:T(8,128)(2,1)}), bf16[64,16,4096]{2,1,0:T(8,128)(2,1)}) %all-gather.2.cloned.1.call-update) | async-done | bytes 8388624 | tf_op jit(solution)/shard_map/all_gather | solution.py:32
  153.9 3.5 %constant_dynamic-slice_fusion = bf16[64,1,4096]{2,1,0:T(2,128)(2,1)S(1)} fusion(bf16[64,16,4096]{2,1,0:T(8,128)(2,1)} %all-gather.2.cloned.1.call-done, s32[]{:T(128)} %bitcast.8), kind=kLoop, calls=%fused_computation.22 | loop fusion | bytes 1048580 | solution.py:32
  157.5 9.2 %fusion.7 = f32[8,8,2048]{2,1,0:T(8,128)S(1)} fusion(bf16[1,4096,2048]{2,1,0:T(8,128)(2,1)} %param.6, bf16[64,1,4096]{2,1,0:T(2,128)(2,1)S(1)} %constant_dynamic-slice_fusion, pred[]{:T(512)} %bitcast.4, f32[]{:T(128)} %bitcast.11), kind=kOutput, calls=%fused_computation.6 | convolution fusion | flops 1074135040 | bytes 17825796 | tf_op jit(solution)/shard_map/rkc,kco->rko/dot_general | solution.py:33
  166.6 0.2 mul.66
  166.9 3.5 %mul.67 = f32[256,1,2048]{2,1,0:T(1,128)} reshape(f32[8,4,8,2048]{3,2,1,0:T(8,128)S(1)} %mul.66) | data formatting | bytes 4194304 | tf_op jit(solution)/shard_map/mul | solution.py:40
  170.4 3.1 %multiply_convert_fusion = bf16[256,1,2048]{2,1,0:T(2,128)(2,1)S(1)} fusion(f32[256,1,2048]{2,1,0:T(1,128)} %mul.67, f32[256]{0:T(256)S(1)} %mul.69), kind=kLoop, calls=%fused_computation.7 | loop fusion | flops 1048576 | bytes 3146752 | tf_op jit(solution)/shard_map/convert_element_type | solution.py:44
  173.5 0.5 broadcast.110
  174.0 7.8 %reduce = bf16[256,2048]{1,0:T(8,128)(2,1)} reduce(bf16[256,1,2048]{2,1,0:T(2,128)(2,1)S(1)} %multiply_convert_fusion, bf16[]{:T(256)} %broadcast.110), dimensions={1}, to_apply=%multiply_convert_fusion.reduce_sub_computation | reduce | bytes 2097154 | tf_op jit(solution)/shard_map/convert_element_type | solution.py:44
  181.8 2.9 %reshape.158 = bf16[32,2,8192]{2,1,0:T(2,128)(2,1)} reshape(bf16[256,2048]{1,0:T(8,128)(2,1)} %reduce) | data formatting | bytes 2097152
  184.7 0.0 all-to-all-done.2
  184.7 2.8 %all-to-all-start.1 = ((bf16[32,2,8192]{2,1,0:T(2,128)(2,1)}), bf16[32,2,8192]{2,1,0:T(2,128)(2,1)S(1)}, u32[]{:S(2)}, u32[]{:S(2)}) async-start(bf16[32,2,8192]{2,1,0:T(2,128)(2,1)} %reshape.158), calls=%async_computation.1 | async-start | bytes 2097152 | tf_op jit(solution)/shard_map/all_to_all | solution.py:43
  187.6 0.6 copy.24
  188.2 1.1 copy.25
  189.3 24.5 %all-to-all-done.1 = bf16[32,2,8192]{2,1,0:T(2,128)(2,1)S(1)} async-done(((bf16[32,2,8192]{2,1,0:T(2,128)(2,1)}), bf16[32,2,8192]{2,1,0:T(2,128)(2,1)S(1)}, u32[]{:S(2)}, u32[]{:S(2)}) %all-to-all-start.1) | async-done | bytes 1048608 | tf_op jit(solution)/shard_map/all_to_all | solution.py:43
  213.7 1.0 reshape.159
  214.8 0.0 copy-start
  214.8 0.6 copy.45
  215.4 0.6 copy-done
  216.0 2.0 fusion.3
  (3 shorter events, 0.0 us)
Async XLA Ops:
  6.5 147.4 %all-gather.2.cloned.1.call-start = ((), (), s32[]{:S(2)}) async-start(), calls=%async_computation.3 | async-start | bytes 9437184 | tf_op jit(solution)/shard_map/all_gather | solution.py:32
  27.9 1.2 slice-start
  28.9 1.2 copy-start.1
  32.2 5.7 %copy-start.2 = (s32[32,2]{0,1:T(2,128)S(1)}, s32[32,2]{0,1:T(2,128)}, u32[]{:S(2)}) copy-start(s32[32,2]{0,1:T(2,128)} %param.8) | copy-start | bytes 772
  32.2 8.9 %copy-start.3 = (s32[32]{0:T(128)S(1)}, s32[32]{0:T(128)}, u32[]{:S(2)}) copy-start(s32[32]{0:T(128)} %param.9) | copy-start | bytes 388
  34.3 150.4 %all-to-all-start.2 = ((f32[2,64,2048]{2,0,1:T(2,128)}), f32[2,64,2048]{2,0,1:T(2,128)S(1)}, u32[]{:S(2)}, u32[]{:S(2)}) async-start(f32[2,64,2048]{2,0,1:T(2,128)} %reshape.157), calls=%async_computation.2 | async-start | bytes 2097152 | tf_op jit(solution)/shard_map/all_to_all | solution.py:31
  184.7 29.0 %all-to-all-start.1 = ((bf16[32,2,8192]{2,1,0:T(2,128)(2,1)}), bf16[32,2,8192]{2,1,0:T(2,128)(2,1)S(1)}, u32[]{:S(2)}, u32[]{:S(2)}) async-start(bf16[32,2,8192]{2,1,0:T(2,128)(2,1)} %reshape.158), calls=%async_computation.1 | async-start | bytes 2097152 | tf_op jit(solution)/shard_map/all_to_all | solution.py:43
  214.8 1.2 copy-start
Sparse Core Ops, SparseCore 0:
  29.1 124.7 all-gather.1
where the time goes:
time: 225 us
  waiting for transfers between devices  135 us (60%)
  local copies, waits for them, and re-layouts  24 us (11%)
  blocking collectives  18.5 us (8%)
  between operations  17.5 us (8%)
  matrix products  12.5 us (6%)
  other arithmetic  10.9 us (5%)
  starting transfers between devices  6.33 us (3%)
    all_gather x1, waiting for transfers between devices, per_device(): lax.all_gather(amps_vm, 'pair', axis=0, tiled=True)  111 us
    all_to_all x1, waiting for transfers between devices, per_device(): lax.all_to_all(outgoing.astype(jnp.bfloat16), ('pair', 'virt'), split_axi...  24.5 us
    all_to_all x1, blocking collectives, per_device(): lax.all_to_all(amps_pm, 'virt', split_axis=1, concat_axis=0, tiled=True)  18.5 us
    convert_element_type x2, other arithmetic, per_device(): outgoing.astype(jnp.bfloat16)  10.9 us
    dot_general x1, matrix products, per_device(): jnp.einsum('rkc,kco->rko', chosen, integrals, preferred_element_type=jnp....  9.16 us
    unnamed x12, local copies, waits for them, and re-layouts  7.49 us
  transfers between devices with their start and end apart: 3, of which 2 were waited for; matrix products, arithmetic and copies ran while one was open for 17% of the time, Pallas kernels for 0%

commit v1 on v0

--- a/solution.py
+++ b/solution.py
@@ -1,12 +1,44 @@
+import functools
 import jax
 import jax.numpy as jnp
 from jax import lax
 from jax.sharding import PartitionSpec as P
+from jax.lax import axis_index, axis_size, ppermute
 
 TILE = 64
 NVT = 8
 A_W = 8
 AS = 32
+
+
+def recast_row(mine, out_dim, xin):
+    u1, g_now = (mine.shape[:out_dim], mine.shape[out_dim + 1 :])
+    seen_now = jnp.moveaxis(mine.reshape(*u1, xin, -1, *g_now), out_dim, 0)
+    return seen_now
+
+
+def _watch_column(m, at_axis):
+    m = jnp.moveaxis(m, 0, at_axis)
+    earlier = m.shape
+    a_next = m.reshape(
+        *earlier[:at_axis], earlier[at_axis] * earlier[at_axis + 1], *earlier[at_axis + 2 :]
+    )
+    return a_next
+
+
+def rest_scales(in_array, axis_name, work_x, point):
+    later, all_rows = (axis_size(axis_name), axis_index(axis_name))
+    t1 = recast_row(in_array, work_x, later)
+    rows = [t1[all_rows]]
+    for pp in range(1, later):
+        v1 = t1[all_rows ^ pp]
+        rows.append(ppermute(v1, axis_name, [(kk, kk ^ pp) for kk in range(later)]))
+    t1 = jnp.stack(rows)[all_rows ^ jnp.arange(later)]
+    x_new = _watch_column(t1, point)
+    return x_new
+
+
+threads_switch = functools.partial(rest_scales, axis_name="virt", work_x=1, point=0)
 
 
 def per_device(amps_pm, integrals, fock_vv, blk_tiles, blk_mask):
@@ -21,7 +53,7 @@
     own_tiles = lax.dynamic_slice_in_dim(blk_tiles, device * blk_dev, blk_dev, 0)
     own_mask = lax.dynamic_slice_in_dim(blk_mask, device * blk_dev, blk_dev, 0).astype(jnp.float32)
     local_in = own_tiles[:, 0] - virt_idx * slab
-    amps_vm = lax.all_to_all(amps_pm, "virt", split_axis=1, concat_axis=0, tiled=True)
+    amps_vm = threads_switch(amps_pm)
     sub_rows = amps_pm[:, :, :out_cols].reshape(pm_rows, A_W, NVT, AS, TILE)
     fock_four = fock_vv.reshape(NVT, TILE, NVT, TILE)
     onebody = jnp.einsum(

time: 225 us -> 218 us (0.969)
  blocking collectives: 18.5 us -> 0 us
  waiting for transfers between devices: 135 us -> 148 us
  local copies, waits for them, and re-layouts: 24 us -> 20 us
  starting transfers between devices: 6.33 us -> 9.52 us
    all_to_all x1 -> x0, blocking collectives: 18.5 us -> none  [per_device(): lax.all_to_all(amps_pm, 'virt', split_axis=1, concat_axis=0, tiled=True)]
    ppermute x0 -> x3, waiting for transfers between devices: none -> 11 us  [rest_scales(): rows.append(ppermute(v1, axis_name, [(kk, kk ^ pp) for kk in range(later)]))]
    another operation x1 -> x0, local copies, waits for them, and re-layouts: 3.53 us -> none  [per_device(): jnp.take(lax.all_gather(amps_vm, 'pair', axis=0, tiled=True), local_in, a...]
    ppermute x0 -> x3, starting transfers between devices: none -> 3.23 us  [rest_scales(): rows.append(ppermute(v1, axis_name, [(kk, kk ^ pp) for kk in range(later)]))]
    unnamed x12 -> x13, local copies, waits for them, and re-layouts: 7.49 us -> 5.21 us
  transfers between devices with their start and end apart: 3 -> 6, of which waited for: 2 -> 4; matrix products, arithmetic and copies ran while one was open for 17% -> 16% of each run, Pallas kernels for 0% -> 0%
where the time goes in v1:
time: 218 us
  waiting for transfers between devices  148 us (68%)
  local copies, waits for them, and re-layouts  20 us (9%)
  between operations  17.5 us (8%)
  matrix products  12.3 us (6%)
  other arithmetic  11.1 us (5%)
  starting transfers between devices  9.52 us (4%)
    all_gather x1, waiting for transfers between devices, per_device(): lax.all_gather(amps_vm, 'pair', axis=0, tiled=True)  112 us
    all_to_all x1, waiting for transfers between devices, per_device(): lax.all_to_all(outgoing.astype(jnp.bfloat16), ('pair', 'virt'), split_axi...  24.5 us
    ppermute x3, waiting for transfers between devices, rest_scales(): rows.append(ppermute(v1, axis_name, [(kk, kk ^ pp) for kk in range(later)]))  11 us
    convert_element_type x2, other arithmetic, per_device(): outgoing.astype(jnp.bfloat16)  10.9 us
    dot_general x1, matrix products, per_device(): jnp.einsum('rkc,kco->rko', chosen, integrals, preferred_element_type=jnp....  8.97 us
    unnamed x13, local copies, waits for them, and re-layouts  5.21 us
  transfers between devices with their start and end apart: 6, of which 4 were waited for; matrix products, arithmetic and copies ran while one was open for 16% of the time, Pallas kernels for 0%

profile of v1, /device:TPU:0, one launch (start us, length us, event | category | flops | bytes accessed | tf_op | source)
XLA Modules:
  0.0 217.9 jit_solution(5115919389593163842)
XLA Ops:
  6.5 0.0 all-gather.2.cloned.1.call-start
  6.5 1.3 dynamic-slice_bitcast_fusion.3
  7.8 3.0 %collective-permute-start.1 = (bf16[2,16,4096]{2,1,0:T(8,128)(2,1)S(1)}, bf16[2,16,4096]{2,1,0:T(8,128)(2,1)S(1)}, u32[]{:S(2)}, u32[]{:S(2)}) collective-permute-start(bf16[2,16,4096]{2,1,0:T(8,128)(2,1)S(1)} %get-tuple-element.17), channel_id=1, source_target_pairs={{0,2},{1,3},{2,0},{3,1},{4,6},{5,7},{6,4},{7,5},{8,10},{9,11},{10,... | collective-permute-start | bytes 786440 | tf_op jit(solution)/shard_map/ppermute | solution.py:35
  10.8 0.0 collective-permute-start.2
  10.8 0.2 collective-permute-start
  11.1 6.9 %collective-permute-done.1 = bf16[2,16,4096]{2,1,0:T(8,128)(2,1)S(1)} collective-permute-done((bf16[2,16,4096]{2,1,0:T(8,128)(2,1)S(1)}, bf16[2,16,4096]{2,1,0:T(8,128)(2,1)S(1)}, u32[]{:S(2)}, u32[]{:S(2)}) %collective-permute-start.1) | collective-permute-done | bytes 262176 | tf_op jit(solution)/shard_map/ppermute | solution.py:35
  18.0 4.0 %collective-permute-done.2 = bf16[2,16,4096]{2,1,0:T(8,128)(2,1)S(1)} collective-permute-done((bf16[2,16,4096]{2,1,0:T(8,128)(2,1)S(1)}, bf16[2,16,4096]{2,1,0:T(8,128)(2,1)S(1)}, u32[]{:S(2)}, u32[]{:S(2)}) %collective-permute-start.2) | collective-permute-done | bytes 262176 | tf_op jit(solution)/shard_map/ppermute | solution.py:35
  22.0 0.0 collective-permute-done
  22.0 0.1 pad_maximum_fusion
  22.2 0.6 gather_fusion
  22.8 0.0 copy-start.1
  22.8 1.5 copy.24
  24.3 0.0 all-gather.2.cloned.1.call-update
  24.4 0.0 copy-done.1
  24.4 1.1 reshape.193
  25.5 0.0 copy-done.2
  25.5 0.5 reshape.142
  26.1 1.3 convolution_bitcast_fusion.1
  27.3 0.2 copy.35
  27.5 0.0 copy-start.3
  27.6 0.0 copy-start.4
  27.6 2.1 reshape.196
  29.7 3.5 %all-to-all-start.1 = ((f32[2,64,2048]{2,0,1:T(2,128)}), f32[2,64,2048]{2,0,1:T(2,128)S(1)}, u32[]{:S(2)}, u32[]{:S(2)}) async-start(f32[2,64,2048]{2,0,1:T(2,128)} %reshape.196), calls=%async_computation.1 | async-start | bytes 2097152 | tf_op jit(solution)/shard_map/all_to_all | solution.py:63
  33.2 0.0 copy-done.3
  33.2 0.1 constant_dynamic-slice_fusion
  33.3 0.6 fusion.25
  36.5 0.0 copy-done.4
  36.5 0.6 dynamic_slice.14
  38.4 0.1 mul.68
  38.5 0.1 mul.69
  38.6 112.1 %all-gather.2.cloned.1.call-done = bf16[64,16,4096]{2,0,1:T(8,128)(2,1)} async-done(((bf16[8,16,4096]{2,0,1:T(8,128)(2,1)}), bf16[64,16,4096]{2,0,1:T(8,128)(2,1)}) %all-gather.2.cloned.1.call-update) | async-done | bytes 8388624 | tf_op jit(solution)/shard_map/all_gather | solution.py:64
  150.7 9.0 %fusion.7 = f32[8,8,2048]{2,1,0:T(8,128)S(1)} fusion(bf16[1,4096,2048]{2,1,0:T(8,128)(2,1)} %param.6, bf16[64,16,4096]{2,0,1:T(8,128)(2,1)} %all-gather.2.cloned.1.call-done, s32[]{:T(128)} %bitcast.15, pred[]{:T(512)} %bitcast.4, f32[]{:T(128)} %bitcast.18), kind=kOutput, calls=%fused_computation.7 | convolution fusion | flops 1074135040 | bytes 17827328 | tf_op jit(solution)/shard_map/rkc,kco->rko/dot_general | solution.py:65
  159.7 0.2 mul.66
  159.9 3.5 %mul.67 = f32[256,1,2048]{2,1,0:T(1,128)} reshape(f32[8,4,8,2048]{3,2,1,0:T(8,128)S(1)} %mul.66) | data formatting | bytes 4194304 | tf_op jit(solution)/shard_map/mul | solution.py:72
  163.4 3.1 %multiply_convert_fusion = bf16[256,1,2048]{2,1,0:T(2,128)(2,1)S(1)} fusion(f32[256,1,2048]{2,1,0:T(1,128)} %mul.67, f32[256]{0:T(256)S(1)} %mul.69), kind=kLoop, calls=%fused_computation.8 | loop fusion | flops 1048576 | bytes 3146752 | tf_op jit(solution)/shard_map/convert_element_type | solution.py:76
  166.6 0.5 broadcast.145
  167.1 7.8 %reduce = bf16[256,2048]{1,0:T(8,128)(2,1)} reduce(bf16[256,1,2048]{2,1,0:T(2,128)(2,1)S(1)} %multiply_convert_fusion, bf16[]{:T(256)} %broadcast.145), dimensions={1}, to_apply=%multiply_convert_fusion.reduce_sub_computation | reduce | bytes 2097154 | tf_op jit(solution)/shard_map/convert_element_type | solution.py:76
  174.9 2.9 %reshape.197 = bf16[32,2,8192]{2,1,0:T(2,128)(2,1)} reshape(bf16[256,2048]{1,0:T(8,128)(2,1)} %reduce) | data formatting | bytes 2097152
  177.8 0.0 all-to-all-done.1
  177.8 2.8 %all-to-all-start = ((bf16[32,2,8192]{2,1,0:T(2,128)(2,1)}), bf16[32,2,8192]{2,1,0:T(2,128)(2,1)S(1)}, u32[]{:S(2)}, u32[]{:S(2)}) async-start(bf16[32,2,8192]{2,1,0:T(2,128)(2,1)} %reshape.197), calls=%async_computation | async-start | bytes 2097152 | tf_op jit(solution)/shard_map/all_to_all | solution.py:75
  180.6 0.6 copy.29
  181.2 1.1 copy.30
  182.3 24.5 %all-to-all-done = bf16[32,2,8192]{2,1,0:T(2,128)(2,1)S(1)} async-done(((bf16[32,2,8192]{2,1,0:T(2,128)(2,1)}), bf16[32,2,8192]{2,1,0:T(2,128)(2,1)S(1)}, u32[]{:S(2)}, u32[]{:S(2)}) %all-to-all-start) | async-done | bytes 1048608 | tf_op jit(solution)/shard_map/all_to_all | solution.py:75
  206.8 1.0 reshape.198
  207.8 0.0 copy-start
  207.8 0.6 copy.49
  208.5 0.6 copy-done
  209.1 2.0 fusion.3
  (7 shorter events, 0.1 us)
Async XLA Ops:
  6.5 144.2 %all-gather.2.cloned.1.call-start = ((), (), s32[]{:S(2)}) async-start(), calls=%async_computation.2 | async-start | bytes 9437184 | tf_op jit(solution)/shard_map/all_gather | solution.py:64
  7.8 10.2 %collective-permute-start.1 = (bf16[2,16,4096]{2,1,0:T(8,128)(2,1)S(1)}, bf16[2,16,4096]{2,1,0:T(8,128)(2,1)S(1)}, u32[]{:S(2)}, u32[]{:S(2)}) collective-permute-start(bf16[2,16,4096]{2,1,0:T(8,128)(2,1)S(1)} %get-tuple-element.17), channel_id=1, source_target_pairs={{0,2},{1,3},{2,0},{3,1},{4,6},{5,7},{6,4},{7,5},{8,10},{9,11},{10,... | collective-permute-start | bytes 786440 | tf_op jit(solution)/shard_map/ppermute | solution.py:35
  10.8 11.2 %collective-permute-start.2 = (bf16[2,16,4096]{2,1,0:T(8,128)(2,1)S(1)}, bf16[2,16,4096]{2,1,0:T(8,128)(2,1)S(1)}, u32[]{:S(2)}, u32[]{:S(2)}) collective-permute-start(bf16[2,16,4096]{2,1,0:T(8,128)(2,1)S(1)} %get-tuple-element.19), channel_id=1, source_target_pairs={{0,3},{1,2},{2,1},{3,0},{4,7},{5,6},{6,5},{7,4},{8,11},{9,10},{10,... | collective-permute-start | bytes 786440 | tf_op jit(solution)/shard_map/ppermute | solution.py:35
  10.8 11.2 %collective-permute-start = (bf16[2,16,4096]{2,1,0:T(8,128)(2,1)S(1)}, bf16[2,16,4096]{2,1,0:T(8,128)(2,1)S(1)}, u32[]{:S(2)}, u32[]{:S(2)}) collective-permute-start(bf16[2,16,4096]{2,1,0:T(8,128)(2,1)S(1)} %get-tuple-element.18), channel_id=1, source_target_pairs={{0,1},{1,0},{2,3},{3,2},{4,5},{5,4},{6,7},{7,6},{8,9},{9,8},{10,11... | collective-permute-start | bytes 786440 | tf_op jit(solution)/shard_map/ppermute | solution.py:35
  22.8 1.6 copy-start.1
  24.3 1.2 copy-start.2
  27.5 5.7 %copy-start.3 = (s32[32,2]{0,1:T(2,128)S(1)}, s32[32,2]{0,1:T(2,128)}, u32[]{:S(2)}) copy-start(s32[32,2]{0,1:T(2,128)} %param.8) | copy-start | bytes 772
  27.6 8.9 %copy-start.4 = (s32[32]{0:T(128)S(1)}, s32[32]{0:T(128)}, u32[]{:S(2)}) copy-start(s32[32]{0:T(128)} %param.9) | copy-start | bytes 388
  29.7 148.1 %all-to-all-start.1 = ((f32[2,64,2048]{2,0,1:T(2,128)}), f32[2,64,2048]{2,0,1:T(2,128)S(1)}, u32[]{:S(2)}, u32[]{:S(2)}) async-start(f32[2,64,2048]{2,0,1:T(2,128)} %reshape.196), calls=%async_computation.1 | async-start | bytes 2097152 | tf_op jit(solution)/shard_map/all_to_all | solution.py:63
  177.8 29.0 %all-to-all-start = ((bf16[32,2,8192]{2,1,0:T(2,128)(2,1)}), bf16[32,2,8192]{2,1,0:T(2,128)(2,1)S(1)}, u32[]{:S(2)}, u32[]{:S(2)}) async-start(bf16[32,2,8192]{2,1,0:T(2,128)(2,1)} %reshape.197), calls=%async_computation | async-start | bytes 2097152 | tf_op jit(solution)/shard_map/all_to_all | solution.py:75
  207.8 1.2 copy-start
Sparse Core Ops, SparseCore 0:
  24.5 126.1 all-gather.1
